TPU v7x, 32 devices: a whole 2x2x4 slice. The times are simulated.
32 devices in a mesh: row: 4 (over x, core), col: 8 (over z, y).
Axes of the slice: x: 2, y: 2, z: 4, core: 2. Of those that a mesh axis runs over, the one named last changes fastest.
Arguments:
- embed: bfloat16 [1024, 768], P(('row', 'col'))
- beta: bfloat16 [1024], P(('row', 'col')), may hold values from 16 to 400
- block_mask: int32 [8, 8], P('row'), may hold values from 0 to 1, as said below
- counts: int32 [8], replicated, may hold values from 2 to 128
- probes: float32 [64, 1024], P(None, ('row', 'col')), may hold values from -6 to 6
Outputs:
- spectral: float32 [64, 1024], P(None, ('row', 'col'))
Inputs may be any that keep to these rules, and one draw needn't show every extreme that they name: `block_mask`: every diagonal entry is 1.
All inputs are finite; a program needn't handle non-finite values.
Results may differ from a plain program's by a relative error of at most 0.012.
The roundings to bfloat16 on the way count: a program that leaves them out, or rounds other values in their place, can miss the bound.
Values may be sent and summed in bfloat16 or wider, within the bound.
No kernel may reach another device: no remote copies, remote signals or barrier semaphores. Data moves between devices by JAX's collectives and lax.ppermute only.
A program may use at most 64 MiB of HBM per device.

v0:
```python
import jax
import jax.numpy as jnp
from jax import lax
from jax.sharding import PartitionSpec as P

ITERS = 2


def spread(shard, axis, root):
    mine = lax.axis_index(axis) == root
    return lax.psum(jnp.where(mine, shard, jnp.zeros_like(shard)), axis)


def own_piece(totals, col_ratio, n_row, row_index, col_index):
    shard_len = totals.shape[1] // n_row
    chosen = jnp.zeros_like(totals)
    for root_k in range(col_ratio):
        received = spread(totals, "col", col_ratio * row_index + root_k)
        chosen = jnp.where(col_index // n_row == root_k, received, chosen)
    return lax.dynamic_slice_in_dim(chosen, col_index % n_row * shard_len, shard_len, 1)


def body(embed, beta, block_mask, counts, probes):
    n_row = lax.axis_size("row")
    n_col = lax.axis_size("col")
    col_ratio = n_col // n_row
    row_index = lax.axis_index("row")
    col_index = lax.axis_index("col")
    shard_len, feat_width = embed.shape
    row_files = shard_len * n_col
    col_files = shard_len * n_row
    values = embed.astype(jnp.float32)
    unit_vec = (
        values * lax.rsqrt(jnp.mean(values * values, axis=1, keepdims=True) + 1e-06)
    ).astype(jnp.bfloat16)
    unit_rows, beta_rows = (
        lax.all_gather(unit_vec, "col", axis=0, tiled=True),
        lax.all_gather(beta, "col", axis=0, tiled=True),
    )
    half_pick = col_index % col_ratio
    col_seq = lax.iota(jnp.int32, col_files)
    unit_cols = spread(
        lax.dynamic_slice_in_dim(unit_rows, half_pick * col_files, col_files, 0),
        "row",
        col_index // col_ratio,
    )
    col_ids = col_index * col_files + col_seq
    gram_tile = lax.dot_general(
        unit_rows, unit_cols, (((1,), (1,)), ((), ())), preferred_element_type=jnp.float32
    )
    scores = gram_tile * (beta_rows.astype(jnp.float32) / feat_width)[:, None]
    row_blocks = block_mask.shape[0]
    blk_size = row_files // row_blocks
    col_block = col_ids // blk_size
    col_live = col_ids % blk_size < jnp.take(counts, col_block, axis=0)
    mask_cols = jnp.take(block_mask, col_block, axis=1) == 1
    block_wide = jnp.broadcast_to(mask_cols[:, None, :], (row_blocks, blk_size, col_files)).reshape(
        row_files, col_files
    )
    row_ids = row_index * row_files + lax.iota(jnp.int32, row_files)
    allowed = block_wide & col_live[None, :] & (row_ids[:, None] != col_ids[None, :])
    masked = jnp.where(allowed, scores, -1e30)
    local_top = jnp.max(masked, axis=1)
    row_top = lax.pmax(local_top, "col")
    row_mass = lax.psum(
        jnp.sum(jnp.where(allowed, jnp.exp(masked - row_top[:, None]), 0.0), axis=1), "col"
    )
    weights = jnp.where(allowed, jnp.exp(masked - row_top[:, None]) / row_mass[:, None], 0.0)
    col_mass = lax.psum(jnp.sum(weights, axis=0), "row")
    own_mass = own_piece(col_mass[None, :], col_ratio, n_row, row_index, col_index)[0]
    inv_root = lax.rsqrt((1.0 + own_mass) * 0.5)
    affinity = weights.astype(jnp.bfloat16)
    probe_state = probes
    for sweep in range(ITERS):
        scaled = (probe_state * inv_root[None, :]).astype(jnp.bfloat16)
        probe_rows = lax.all_gather(scaled, "col", axis=1, tiled=True)
        probe_cols = spread(
            lax.dynamic_slice_in_dim(probe_rows, half_pick * col_files, col_files, 1),
            "row",
            col_index // col_ratio,
        )
        row_part = lax.dot_general(
            probe_cols, affinity, (((1,), (1,)), ((), ())), preferred_element_type=jnp.float32
        )
        col_part = jnp.dot(probe_rows, affinity, preferred_element_type=jnp.float32)
        own_rows = lax.psum_scatter(
            row_part.astype(jnp.bfloat16), "col", scatter_dimension=1, tiled=True
        ).astype(jnp.float32)
        col_total = lax.psum(col_part, "row")
        own_cols = own_piece(col_total, col_ratio, n_row, row_index, col_index)
        probe_state = (own_rows + own_cols) * (0.5 * inv_root)[None, :]
    return probe_state


def solution(mesh):
    placed = (
        P(("row", "col"), None),
        P(("row", "col")),
        P("row", None),
        P(),
        P(None, ("row", "col")),
    )
    return jax.shard_map(
        body, mesh=mesh, in_specs=placed, out_specs=P(None, ("row", "col")), check_vma=False
    )
```

profile of v0, /device:TPU:0, one launch (start us, length us, event | category | flops | bytes accessed | tf_op | source)
XLA Modules:
  0.0 495.1 jit_solution(6957773946014642195)
XLA Ops:
  6.5 0.8 copy-done
  7.5 32.7 %all_gather.12 = bf16[256,768]{1,0:T(8,128)(2,1)S(1)} all-gather(bf16[32,768]{1,0:T(8,128)(2,1)S(1)} %fusion.2), channel_id=1, replica_groups=mesh['row'=4,'col'=8] {'col'}, dimensions={0}, use_global_device_ids=true | all-gather | bytes 442368 | tf_op jit(solution)/shard_map/all_gather | solution.py:37
  40.3 0.7 dynamic-slice_select_fusion
  41.2 0.6 copy-done.1
  41.8 0.7 fusion.21
  42.5 0.7 copy-done.3
  43.3 0.6 gather_fusion
  44.3 0.6 copy-done.5
  46.2 0.6 copy-done.4
  47.0 21.5 %all-reduce = bf16[256]{0:T(256)(128)(2,1)S(1)} all-reduce(bf16[256]{0:T(256)(128)(2,1)S(1)} %dynamic-update-slice), channel_id=1, replica_groups=mesh['row'=4,'col'=8] {'col'}, use_global_device_ids=true, to_apply=%add | all-reduce | flops 256 | bytes 1024
  68.5 5.1 %fusion.12 = pred[128]{0:T(512)(128)(4,1)S(1)} fusion(s32[]{:T(128)} %bitcast.3, s32[]{:T(128)} %bitcast.4, s32[]{:T(128)} %bitcast.5, s32[]{:T(128)} %bitcast.6, s32[]{:T(128)} %bitcast.7, s32[]{:T(128)} %bitcast.8, s32[]{:T(128)} %bitcast.9, s32[]{:T(128)} %bitcast.10, s32[]{:T(128)S(6)} %mul.86), kind=kLoop, calls=%fused_computation.62 | loop fusion | flops 7808 | bytes 164 | tf_op jit(solution)/shard_map/lt | solution.py:55
  74.0 1.2 fusion.22
  75.2 21.3 %pmax.7 = f32[256]{0:T(256)S(1)} all-reduce(f32[256]{0:T(256)S(1)} %get-tuple-element.29), channel_id=1, replica_groups=mesh['row'=4,'col'=8] {'col'}, use_global_device_ids=true, to_apply=%region_3.4 | all-reduce | flops 256 | bytes 2048 | tf_op jit(solution)/shard_map/pmax | solution.py:64
  96.7 17.1 %psum.92 = f32[256]{0:T(256)S(1)} all-reduce(f32[256]{0:T(256)S(1)} %select_reduce_fusion), channel_id=1, replica_groups=mesh['row'=4,'col'=8] {'col'}, use_global_device_ids=true, to_apply=%region_5.6 | all-reduce | flops 256 | bytes 2048 | tf_op jit(solution)/shard_map/psum | solution.py:65
  114.0 5.9 %psum.93 = f32[128]{0:T(128)S(1)} all-reduce(f32[128]{0:T(128)S(1)} %get-tuple-element.13), channel_id=1, replica_groups=mesh['row'=4,'col'=8] {'row'}, use_global_device_ids=true, to_apply=%region_7.8 | all-reduce | flops 128 | bytes 1024 | tf_op jit(solution)/shard_map/psum | solution.py:69
  119.9 19.1 %all-reduce.3 = (f32[1,128]{1,0:T(1,128)S(1)}, f32[1,128]{1,0:T(1,128)S(1)}) all-reduce(f32[1,128]{1,0:T(1,128)S(1)} %get-tuple-element.20, f32[1,128]{1,0:T(1,128)S(1)} %get-tuple-element.19), channel_id=1, replica_groups=mesh['row'=4,'col'=8] {'col'}, use_global_device_ids=true, to_apply=%region_8.9 | all-reduce | flops 256 | bytes 2048 | tf_op jit(solution)/shard_map/psum | solution.py:11
  139.2 30.5 %all_gather.14 = bf16[64,256]{0,1:T(8,128)(2,1)S(1)} all-gather(bf16[64,32]{0,1:T(8,128)(2,1)S(1)} %multiply_convert_fusion), channel_id=1, replica_groups=mesh['row'=4,'col'=8] {'col'}, dimensions={1}, use_global_device_ids=true | all-gather | bytes 36864 | tf_op jit(solution)/shard_map/all_gather | solution.py:76
  169.7 10.3 %psum.96 = bf16[64,128]{0,1:T(8,128)(2,1)S(1)} all-reduce(bf16[64,128]{0,1:T(8,128)(2,1)S(1)} %dynamic-slice_select_fusion.2), channel_id=1, replica_groups=mesh['row'=4,'col'=8] {'row'}, use_global_device_ids=true, to_apply=%region_10.11 | all-reduce | flops 8192 | bytes 32768 | tf_op jit(solution)/shard_map/psum | solution.py:11
  180.1 0.8 convolution_convert_fusion.1
  181.0 10.7 %psum.97 = f32[64,128]{0,1:T(8,128)S(1)} all-reduce(f32[64,128]{0,1:T(8,128)S(1)} %fusion.23), channel_id=1, replica_groups=mesh['row'=4,'col'=8] {'row'}, use_global_device_ids=true, to_apply=%region_12.13 | all-reduce | flops 8192 | bytes 65536 | tf_op jit(solution)/shard_map/psum | solution.py:89
  191.8 0.7 broadcast_select_fusion.2
  192.5 46.2 %reduce-scatter.3.cloned.1.call-done = bf16[64,32]{0,1:T(8,128)(2,1)} async-done(((bf16[64,256]{0,1:T(8,128)(2,1)}), bf16[64,32]{0,1:T(8,128)(2,1)}) %reduce-scatter.3.cloned.1.call-update) | async-done | bytes 4112 | tf_op jit(solution)/shard_map/reduce_scatter | solution.py:86
  238.7 72.8 %all-reduce.12.cloned.1.call-done = (f32[64,128]{0,1:T(8,128)}, f32[64,128]{0,1:T(8,128)}) async-done(((f32[64,128]{0,1:T(8,128)}, f32[64,128]{0,1:T(8,128)}), (f32[64,128]{0,1:T(8,128)}, f32[64,128]{0,1:T(8,128)})) %all-reduce.12.cloned.1.call-update) | async-done | bytes 65552 | tf_op jit(solution)/shard_map/psum | solution.py:11
  311.5 0.8 fusion.9
  312.3 30.5 %all_gather.15 = bf16[64,256]{0,1:T(8,128)(2,1)S(1)} all-gather(bf16[64,32]{0,1:T(8,128)(2,1)S(1)} %fusion.9), channel_id=1, replica_groups=mesh['row'=4,'col'=8] {'col'}, dimensions={1}, use_global_device_ids=true | all-gather | bytes 36864 | tf_op jit(solution)/shard_map/all_gather | solution.py:76
  343.0 10.3 %psum.100 = bf16[64,128]{0,1:T(8,128)(2,1)S(1)} all-reduce(bf16[64,128]{0,1:T(8,128)(2,1)S(1)} %dynamic-slice_select_fusion.1), channel_id=1, replica_groups=mesh['row'=4,'col'=8] {'row'}, use_global_device_ids=true, to_apply=%region_15.16 | all-reduce | flops 8192 | bytes 32768 | tf_op jit(solution)/shard_map/psum | solution.py:11
  353.3 0.8 convolution_convert_fusion
  354.2 11.8 %psum.101 = f32[64,128]{0,1:T(8,128)S(1)} all-reduce(f32[64,128]{0,1:T(8,128)S(1)} %fusion.24), channel_id=1, replica_groups=mesh['row'=4,'col'=8] {'row'}, use_global_device_ids=true, to_apply=%region_17.18 | all-reduce | flops 8192 | bytes 65536 | tf_op jit(solution)/shard_map/psum | solution.py:89
  366.0 0.7 broadcast_select_fusion.1
  366.7 48.3 %reduce-scatter.5.cloned.1.call-done = bf16[64,32]{0,1:T(8,128)(2,1)} async-done(((bf16[64,256]{0,1:T(8,128)(2,1)}), bf16[64,32]{0,1:T(8,128)(2,1)}) %reduce-scatter.5.cloned.1.call-update) | async-done | bytes 4112 | tf_op jit(solution)/shard_map/reduce_scatter | solution.py:86
  415.0 72.3 %all-reduce.10.cloned.1.call-done = (f32[64,128]{0,1:T(8,128)}, f32[64,128]{0,1:T(8,128)}) async-done(((f32[64,128]{0,1:T(8,128)}, f32[64,128]{0,1:T(8,128)}), (f32[64,128]{0,1:T(8,128)}, f32[64,128]{0,1:T(8,128)})) %all-reduce.10.cloned.1.call-update) | async-done | bytes 65552 | tf_op jit(solution)/shard_map/psum | solution.py:11
  487.2 1.4 fusion.5
  (45 shorter events, 2.8 us)
Async XLA Ops:
  6.5 0.8 copy-start
  6.5 67.5 %all-reduce.8.cloned.1.call-start = ((), (), s32[]{:S(2)}) async-start(), calls=%async_computation.2 | async-start | bytes 393216 | tf_op jit(solution)/shard_map/psum | solution.py:11
  41.0 197.7 %reduce-scatter.3.cloned.1.call-start = ((), (), s32[]{:S(2)}) async-start(), calls=%async_computation.3 | async-start | bytes 73728 | tf_op jit(solution)/shard_map/reduce_scatter | solution.py:86
  41.2 0.7 copy-start.1
  42.5 0.7 copy-start.3
  44.2 0.7 copy-start.5
  46.1 0.7 copy-start.4
  114.0 25.1 %copy-start.2 = (f32[64,32]{0,1:T(8,128)S(1)}, f32[64,32]{0,1:T(8,128)}, u32[]{:S(2)}) copy-start(f32[64,32]{0,1:T(8,128)} %param.9) | copy-start | bytes 24580
  181.0 130.5 %all-reduce.12.cloned.1.call-start = ((), (), s32[]{:S(2)}) async-start(), calls=%async_computation.6 | async-start | bytes 262144 | tf_op jit(solution)/shard_map/psum | solution.py:11
  192.4 222.5 %reduce-scatter.5.cloned.1.call-start = ((), (), s32[]{:S(2)}) async-start(), calls=%async_computation.4 | async-start | bytes 73728 | tf_op jit(solution)/shard_map/reduce_scatter | solution.py:86
  354.1 133.1 %all-reduce.10.cloned.1.call-start = ((), (), s32[]{:S(2)}) async-start(), calls=%async_computation.5 | async-start | bytes 262144 | tf_op jit(solution)/shard_map/psum | solution.py:11
Sparse Core Ops, SparseCore 0:
  41.1 32.8 all-reduce.7
  181.1 57.5 reduce-scatter.2
  242.6 68.8 all-reduce.11
  354.3 60.6 reduce-scatter.4
  418.3 68.8 all-reduce.9
where the time goes:
time: 496 us; the launch traced here: 495 us
  waiting for transfers between devices  240 us (48%)
  blocking collectives  222 us (45%)
  between operations  14 us (3%)
  other arithmetic  10.2 us (2%)
  local copies, waits for them, and re-layouts  5.8 us (1%)
    psum x3, waiting for transfers between devices, spread(): return lax.psum(jnp.where(mine, shard, jnp.zeros_like(shard)), axis)  145 us
    reduce_scatter x2, waiting for transfers between devices, body(): lax.psum_scatter(row_part.astype(jnp.bfloat16), 'col', scatter_dimension=...  94.5 us
    all_gather x2, blocking collectives, body(): probe_rows = lax.all_gather(scaled, 'col', axis=1, tiled=True)  61 us
    psum x3, blocking collectives, spread(): return lax.psum(jnp.where(mine, shard, jnp.zeros_like(shard)), axis)  39.7 us
    all_gather x1, blocking collectives, body(): lax.all_gather(unit_vec, 'col', axis=0, tiled=True)  32.7 us
    psum x2, blocking collectives, body(): col_total = lax.psum(col_part, 'row')  22.5 us
    unnamed x1, blocking collectives  21.5 us
    pmax x1, blocking collectives, body(): row_top = lax.pmax(local_top, 'col')  21.3 us
  transfers between devices with their start and end apart: 5, of which 5 were waited for; matrix products, arithmetic and copies ran while one was open for 2% of the time, Pallas kernels for 0%

commit v1 on v0

--- a/solution.py
+++ b/solution.py
@@ -8,7 +8,7 @@
 
 def spread(shard, axis, root):
     mine = lax.axis_index(axis) == root
-    return lax.psum(jnp.where(mine, shard, jnp.zeros_like(shard)), axis)
+    return jnp.sum(lax.all_gather(jnp.where(mine, shard, jnp.zeros_like(shard)), axis), axis=0)
 
 
 def own_piece(totals, col_ratio, n_row, row_index, col_index):

time: 496 us -> 389 us (0.78)
  waiting for transfers between devices: 240 us -> 0.04 us
  blocking collectives: 222 us -> 358 us
    all_gather x0 -> x9, blocking collectives: none -> 177 us  [spread(): lax.all_gather(jnp.where(mine, shard, jnp.zeros_like(shard)), axis)]
    psum x3 -> x0, waiting for transfers between devices: 145 us -> none  [spread(): return lax.psum(jnp.where(mine, shard, jnp.zeros_like(shard)), axis)]
    reduce_scatter x2, waiting for transfers between devices: 94.5 us -> 0.01 us  [body(): lax.psum_scatter(row_part.astype(jnp.bfloat16), 'col', scatter_dimension=...]
    psum x3 -> x0, blocking collectives: 39.7 us -> none  [spread(): return lax.psum(jnp.where(mine, shard, jnp.zeros_like(shard)), axis)]
  transfers between devices with their start and end apart: 5 -> 2, of which waited for: 5 -> 0; matrix products, arithmetic and copies ran while one was open for 2% -> 0% of each run, Pallas kernels for 0% -> 0%
where the time goes in v1:
time: 389 us
  blocking collectives  358 us (92%)
  between operations  14.3 us (4%)
  other arithmetic  8.36 us (2%)
  local copies, waits for them, and re-layouts  5.87 us (2%)
    all_gather x9, blocking collectives, spread(): lax.all_gather(jnp.where(mine, shard, jnp.zeros_like(shard)), axis)  177 us
    all_gather x2, blocking collectives, body(): probe_rows = lax.all_gather(scaled, 'col', axis=1, tiled=True)  61 us
    all_gather x1, blocking collectives, body(): lax.all_gather(unit_vec, 'col', axis=0, tiled=True)  32.7 us
    psum x2, blocking collectives, body(): col_total = lax.psum(col_part, 'row')  23.5 us
    unnamed x1, blocking collectives  21.5 us
    psum x1, blocking collectives, body(): lax.psum(jnp.sum(jnp.where(allowed, jnp.exp(masked - row_top[:, None]), 0...  19.1 us
    pmax x1, blocking collectives, body(): row_top = lax.pmax(local_top, 'col')  17.1 us
  transfers between devices with their start and end apart: 2, of which 0 were waited for; matrix products, arithmetic and copies ran while one was open for 0% of the time, Pallas kernels for 0%

profile of v1, /device:TPU:0, one launch (start us, length us, event | category | flops | bytes accessed | tf_op | source)
XLA Modules:
  0.0 388.6 jit_solution(4492221853647805082)
XLA Ops:
  6.7 0.7 copy-done
  7.5 32.7 %all_gather.66 = bf16[256,768]{1,0:T(8,128)(2,1)S(1)} all-gather(bf16[32,768]{1,0:T(8,128)(2,1)S(1)} %fusion.2), channel_id=1, replica_groups=mesh['row'=4,'col'=8] {'col'}, dimensions={0}, use_global_device_ids=true | all-gather | bytes 442368 | tf_op jit(solution)/shard_map/all_gather | solution.py:37
  40.3 8.6 %all-gather = bf16[512,768]{1,0:T(8,128)(2,1)S(1)} all-gather(bf16[128,768]{1,0:T(8,128)(2,1)S(1)} %dynamic-slice_select_fusion), channel_id=2, replica_groups=mesh['row'=4,'col'=8] {'row'}, dimensions={0}, use_global_device_ids=true | all-gather | bytes 983040 | tf_op jit(solution)/shard_map/all_gather | solution.py:11
  48.9 0.7 fusion.11
  49.6 0.7 copy-done.3
  50.4 0.6 gather_fusion
  51.5 0.5 copy-done.5
  52.0 0.6 dynamic-slice.4
  53.3 0.6 copy-done.4
  53.9 0.2 dynamic-update-slice
  54.1 21.5 %all-reduce = bf16[256]{0:T(256)(128)(2,1)S(1)} all-reduce(bf16[256]{0:T(256)(128)(2,1)S(1)} %dynamic-update-slice), channel_id=1, replica_groups=mesh['row'=4,'col'=8] {'col'}, use_global_device_ids=true, to_apply=%add | all-reduce | flops 256 | bytes 1024
  75.6 5.0 %fusion.6 = pred[128]{0:T(512)(128)(4,1)S(1)} fusion(s32[]{:T(128)} %bitcast.3, s32[]{:T(128)} %bitcast.4, s32[]{:T(128)} %bitcast.5, s32[]{:T(128)} %bitcast.6, s32[]{:T(128)} %bitcast.7, s32[]{:T(128)} %bitcast.8, s32[]{:T(128)} %bitcast.9, s32[]{:T(128)} %bitcast.10, s32[]{:T(128)S(6)} %mul.89), kind=kLoop, calls=%fused_computation.57 | loop fusion | flops 7808 | bytes 164 | tf_op jit(solution)/shard_map/lt | solution.py:55
  80.6 0.3 fusion.12
  80.9 17.1 %pmax.7 = f32[256]{0:T(256)S(1)} all-reduce(f32[256]{0:T(256)S(1)} %get-tuple-element.23), channel_id=1, replica_groups=mesh['row'=4,'col'=8] {'col'}, use_global_device_ids=true, to_apply=%region_3.4 | all-reduce | flops 256 | bytes 2048 | tf_op jit(solution)/shard_map/pmax | solution.py:64
  98.2 19.1 %psum.28 = f32[256]{0:T(256)S(1)} all-reduce(f32[256]{0:T(256)S(1)} %select_reduce_fusion), channel_id=1, replica_groups=mesh['row'=4,'col'=8] {'col'}, use_global_device_ids=true, to_apply=%region_5.6 | all-reduce | flops 256 | bytes 2048 | tf_op jit(solution)/shard_map/psum | solution.py:65
  117.5 5.9 %psum.29 = f32[128]{0:T(128)S(1)} all-reduce(f32[128]{0:T(128)S(1)} %get-tuple-element.7), channel_id=1, replica_groups=mesh['row'=4,'col'=8] {'row'}, use_global_device_ids=true, to_apply=%region_7.8 | all-reduce | flops 128 | bytes 1024 | tf_op jit(solution)/shard_map/psum | solution.py:69
  123.4 16.3 %all-gather.9 = f32[8,1,128]{2,1,0:T(1,128)S(1)} all-gather(f32[1,1,128]{2,1,0:T(1,128)S(1)} %get-tuple-element.14), channel_id=3, replica_groups=mesh['row'=4,'col'=8] {'col'}, dimensions={0}, use_global_device_ids=true | all-gather | bytes 4608 | tf_op jit(solution)/shard_map/all_gather | solution.py:11
  139.7 18.2 %all-gather.10 = f32[8,1,128]{2,1,0:T(1,128)S(1)} all-gather(f32[1,1,128]{2,1,0:T(1,128)S(1)} %get-tuple-element.13), channel_id=4, replica_groups=mesh['row'=4,'col'=8] {'col'}, dimensions={0}, use_global_device_ids=true | all-gather | bytes 4608 | tf_op jit(solution)/shard_map/all_gather | solution.py:11
  158.1 30.5 %all_gather.74 = bf16[64,256]{0,1:T(8,128)(2,1)S(1)} all-gather(bf16[64,32]{0,1:T(8,128)(2,1)S(1)} %multiply_convert_fusion.1), channel_id=1, replica_groups=mesh['row'=4,'col'=8] {'col'}, dimensions={1}, use_global_device_ids=true | all-gather | bytes 36864 | tf_op jit(solution)/shard_map/all_gather | solution.py:76
  188.7 5.2 %all-gather.3 = bf16[256,128]{1,0:T(8,128)(2,1)S(1)} all-gather(bf16[64,128]{1,0:T(8,128)(2,1)S(1)} %copy.23), channel_id=5, replica_groups=mesh['row'=4,'col'=8] {'row'}, dimensions={0}, use_global_device_ids=true | all-gather | bytes 81920 | tf_op jit(solution)/shard_map/all_gather | solution.py:11
  194.0 0.8 convolution_convert_fusion.1
  195.0 10.9 %psum.30 = f32[64,128]{0,1:T(8,128)S(1)} all-reduce(f32[64,128]{0,1:T(8,128)S(1)} %fusion.13), channel_id=1, replica_groups=mesh['row'=4,'col'=8] {'row'}, use_global_device_ids=true, to_apply=%region_12.13 | all-reduce | flops 8192 | bytes 65536 | tf_op jit(solution)/shard_map/psum | solution.py:89
  206.1 30.8 %all-gather.5 = f32[512,128]{1,0:T(8,128)S(1)} all-gather(f32[64,128]{1,0:T(8,128)S(1)} %copy.26), channel_id=7, replica_groups=mesh['row'=4,'col'=8] {'col'}, dimensions={0}, use_global_device_ids=true | all-gather | bytes 294912 | tf_op jit(solution)/shard_map/all_gather | solution.py:11
  237.1 30.8 %all-gather.4 = f32[512,128]{1,0:T(8,128)S(1)} all-gather(f32[64,128]{1,0:T(8,128)S(1)} %copy.25), channel_id=6, replica_groups=mesh['row'=4,'col'=8] {'col'}, dimensions={0}, use_global_device_ids=true | all-gather | bytes 294912 | tf_op jit(solution)/shard_map/all_gather | solution.py:11
  268.1 0.8 multiply_convert_fusion
  268.8 30.5 %all_gather.81 = bf16[64,256]{0,1:T(8,128)(2,1)S(1)} all-gather(bf16[64,32]{0,1:T(8,128)(2,1)S(1)} %multiply_convert_fusion), channel_id=1, replica_groups=mesh['row'=4,'col'=8] {'col'}, dimensions={1}, use_global_device_ids=true | all-gather | bytes 36864 | tf_op jit(solution)/shard_map/all_gather | solution.py:76
  299.6 5.3 %all-gather.6 = bf16[256,128]{1,0:T(8,128)(2,1)S(1)} all-gather(bf16[64,128]{1,0:T(8,128)(2,1)S(1)} %copy.29), channel_id=8, replica_groups=mesh['row'=4,'col'=8] {'row'}, dimensions={0}, use_global_device_ids=true | all-gather | bytes 81920 | tf_op jit(solution)/shard_map/all_gather | solution.py:11
  304.9 0.8 convolution_convert_fusion
  305.8 12.6 %psum.31 = f32[64,128]{0,1:T(8,128)S(1)} all-reduce(f32[64,128]{0,1:T(8,128)S(1)} %fusion.14), channel_id=1, replica_groups=mesh['row'=4,'col'=8] {'row'}, use_global_device_ids=true, to_apply=%region_17.18 | all-reduce | flops 8192 | bytes 65536 | tf_op jit(solution)/shard_map/psum | solution.py:89
  318.4 30.8 %all-gather.7 = f32[512,128]{1,0:T(8,128)S(1)} all-gather(f32[64,128]{1,0:T(8,128)S(1)} %copy.31), channel_id=9, replica_groups=mesh['row'=4,'col'=8] {'col'}, dimensions={0}, use_global_device_ids=true | all-gather | bytes 294912 | tf_op jit(solution)/shard_map/all_gather | solution.py:11
  349.3 30.8 %all-gather.8 = f32[512,128]{1,0:T(8,128)S(1)} all-gather(f32[64,128]{1,0:T(8,128)S(1)} %copy.32), channel_id=10, replica_groups=mesh['row'=4,'col'=8] {'col'}, dimensions={0}, use_global_device_ids=true | all-gather | bytes 294912 | tf_op jit(solution)/shard_map/all_gather | solution.py:11
  380.3 1.4 add_multiply_fusion
  (64 shorter events, 2.8 us)
Async XLA Ops:
  6.5 261.5 %reduce-scatter.3.cloned.1.call-start = ((), (), s32[]{:S(2)}) async-start(), calls=%async_computation.2 | async-start | bytes 73728 | tf_op jit(solution)/shard_map/reduce_scatter | solution.py:86
  6.5 0.8 copy-start
  40.3 8.6 %copy-start.1 = (s32[8]{0:T(128)S(1)}, s32[8]{0:T(128)}, u32[]{:S(2)}) copy-start(s32[8]{0:T(128)} %param.8) | copy-start | bytes 100
  49.6 0.7 copy-start.3
  51.4 0.7 copy-start.5
  53.3 0.7 copy-start.4
  123.4 34.6 %copy-start.2 = (f32[64,32]{0,1:T(8,128)S(1)}, f32[64,32]{0,1:T(8,128)}, u32[]{:S(2)}) copy-start(f32[64,32]{0,1:T(8,128)} %param.9) | copy-start | bytes 24580
  194.8 185.5 %reduce-scatter.5.cloned.1.call-start = ((), (), s32[]{:S(2)}) async-start(), calls=%async_computation.3 | async-start | bytes 73728 | tf_op jit(solution)/shard_map/reduce_scatter | solution.py:86
Sparse Core Ops, SparseCore 0:
  194.9 57.5 reduce-scatter.2
  305.9 59.0 reduce-scatter.4
